TPU v7x, 32 devices: a whole 2x2x4 slice. The times are simulated.
32 devices in a mesh: dom: 2 (over y), blk: 16 (over z, x, core).
Axes of the slice: x: 2, y: 2, z: 4, core: 2. Of those that a mesh axis runs over, the one named last changes fastest.
Arguments:
- right_side: float32 [2, 4, 2, 8192], P(None, None, 'dom', 'blk')
- near_blocks: bfloat16 [2, 32, 4, 2, 256, 256], P('dom', 'blk'), may hold values from -0.125 to 0.125
- near_cols: int32 [2, 32, 4], P('dom', 'blk'), may hold values from 0 to 5
- partner: int32 [2, 32], P('dom', 'blk'), may hold values from 0 to 3, as said below
- source_basis: bfloat16 [2, 2, 64, 8192], P('dom', None, None, 'blk'), may hold values from -0.25 to 0.25
- target_basis: bfloat16 [2, 2, 64, 8192], P('dom', None, None, 'blk'), may hold values from -0.75 to 0.75
- coupling: float32 [2, 16, 16, 2, 64, 64], P('dom', 'blk'), as said below
- far_ranks: int32 [2, 16, 16], P('dom', 'blk'), may hold values from 32 to 64, as said below
Outputs:
- second_basis: float32 [2, 4, 2, 8192], P(None, None, 'dom', 'blk')
- third_basis: float32 [2, 4, 2, 8192], P(None, None, 'dom', 'blk')
- hessenberg: float32 [4, 9], replicated
Inputs may be any that keep to these rules, and one draw needn't show every extreme that they name: partner[d, c * 2 + i] = e * 2 + j names block j of cluster c in subdomain e; the named block names the first one back, and no block names itself. coupling[d, c, s, a, k, l] equals coupling[d, s, c, a, l, k]. far_ranks[d, c, s] equals far_ranks[d, s, c].
All inputs are finite; a program needn't handle non-finite values.
Results may differ from a plain program's by a relative error of at most 0.0065.
Values may be sent and summed in bfloat16 or wider, within the bound.
No kernel may reach another device: no remote copies, remote signals or barrier semaphores. Data moves between devices by JAX's collectives and lax.ppermute only.
A program may use at most 64 MiB of HBM per device.

v0:
```python
import jax
import jax.numpy as jnp
from jax import lax
from jax.sharding import PartitionSpec as P

EPSILON = 1e-06


def extended(cells, sides, width):
    for axis, dim in sides:
        count = lax.axis_size(axis)
        ends = count - 1
        head = lax.slice_in_dim(cells, 0, width, axis=dim)
        tail = lax.slice_in_dim(cells, cells.shape[dim] - width, cells.shape[dim], axis=dim)
        cells = jnp.concatenate(
            [
                lax.ppermute(tail, axis, [(i, (i + 1) % count) for i in range(ends)]),
                cells,
                lax.ppermute(head, axis, [((i + 1) % count, i) for i in range(ends)]),
            ],
            axis=dim,
        )
    return cells


def complex_mix(products):
    return jnp.stack([products[0, 0] - products[1, 1], products[0, 1] + products[1, 0]])


def apply_operator(
    vector, near_blocks, near_cols, partner, source_basis, target_basis, coupling, far_ranks
):
    nrhs = vector.shape[1]
    rows = vector.shape[3]
    blocks_dev = near_blocks.shape[1]
    slots = near_blocks.shape[2]
    width = near_blocks.shape[4]
    rank_cap = source_basis.shape[2]
    rounded = vector.astype(jnp.bfloat16)
    window = extended(rounded, (("blk", 3),), rows)
    window = window.reshape(2, nrhs, 3 * blocks_dev, width)
    chosen = jnp.take(window, near_cols[0].reshape(-1), axis=2).reshape(
        2, nrhs, blocks_dev, slots, width
    )
    near_prod = jnp.einsum(
        "ikarc,pqikc->apqir", near_blocks[0], chosen, preferred_element_type=jnp.float32
    )
    near_part = complex_mix(near_prod).reshape(2, nrhs, 1, rows)
    coef_prod = jnp.einsum(
        "akr,pqr->apqk", source_basis[0], rounded[:, :, 0], preferred_element_type=jnp.float32
    )
    coeffs = jnp.stack([coef_prod[0, 0] + coef_prod[1, 1], coef_prod[0, 1] - coef_prod[1, 0]])
    row_coupling = coupling[0, 0]
    row_ranks = far_ranks[0, 0]
    levels = jnp.arange(rank_cap, dtype=jnp.int32)
    limit = row_ranks[:, None, None]
    keep = (levels[None, :, None] < limit) & (levels[None, None, :] < limit)
    weights = row_coupling * keep[:, None].astype(jnp.float32)
    inner = jnp.einsum(
        "sakl,spql->apqk",
        weights,
        lax.all_gather(coeffs[None], "blk", axis=0, tiled=True),
        precision=lax.Precision.HIGHEST,
    )
    far_coef = complex_mix(inner)
    rounded_coef = far_coef.astype(jnp.bfloat16)
    outward = jnp.einsum(
        "akr,pqk->apqr", target_basis[0], rounded_coef, preferred_element_type=jnp.float32
    )
    far_part = complex_mix(outward).reshape(2, nrhs, 1, rows)
    every = lax.all_gather(vector, "dom", axis=2, tiled=True)
    every = every.reshape(2, nrhs, -1, width)
    mates = jnp.take(every, partner[0], axis=2).reshape(2, nrhs, 1, rows)
    return vector + near_part + far_part - mates


def local_products(vectors, image):
    stacked = []
    for basis in vectors:
        real_part = jnp.sum(basis[0] * image[0] + basis[1] * image[1], axis=(1, 2))
        imag_part = jnp.sum(basis[0] * image[1] - basis[1] * image[0], axis=(1, 2))
        stacked.append(jnp.stack([real_part, imag_part]))
    return jnp.stack(stacked)


def local_squares(field):
    return jnp.sum(field[0] * field[0] + field[1] * field[1], axis=(1, 2))


def scaled(factor, field):
    real_f = factor[0][:, None, None]
    imag_f = factor[1][:, None, None]
    return jnp.stack([real_f * field[0] - imag_f * field[1], real_f * field[1] + imag_f * field[0]])


def shards(
    right_side, near_blocks, near_cols, partner, source_basis, target_basis, coupling, far_ranks
):
    rows = right_side.shape[3]
    total = float(rows * lax.axis_size("dom") * lax.axis_size("blk"))

    def operator(field):
        return apply_operator(
            field, near_blocks, near_cols, partner, source_basis, target_basis, coupling, far_ranks
        )

    start_sum = lax.psum(local_squares(right_side), ("dom", "blk"))
    beta = jnp.sqrt(start_sum / total + EPSILON)
    first_vec = right_side / beta[None, :, None, None]
    image_one = operator(first_vec)

    def projections(vectors, image):
        return lax.psum(local_products(vectors, image), ("dom", "blk")) / total

    def lengths(field):
        return lax.psum(local_squares(field), ("dom", "blk")) / total

    h_one_one = projections([first_vec], image_one)[0]
    rest_one = image_one - scaled(h_one_one, first_vec)
    h_two_one = jnp.sqrt(lengths(rest_one) + EPSILON)
    second_basis = rest_one / h_two_one[None, :, None, None]
    image_two = operator(second_basis)
    both = projections([first_vec, second_basis], image_two)
    h_one_two = both[0]
    h_two_two = both[1]
    rest_two = image_two - scaled(h_one_two, first_vec) - scaled(h_two_two, second_basis)
    h_three_two = jnp.sqrt(lengths(rest_two) + EPSILON)
    third_basis = rest_two / h_three_two[None, :, None, None]
    hessenberg = jnp.stack(
        [
            beta,
            h_one_one[0],
            h_one_one[1],
            h_two_one,
            h_one_two[0],
            h_one_two[1],
            h_two_two[0],
            h_two_two[1],
            h_three_two,
        ],
        axis=1,
    )
    return (second_basis, third_basis, hessenberg)


def solution(mesh):
    return jax.shard_map(
        shards,
        mesh=mesh,
        in_specs=(
            P(None, None, "dom", "blk"),
            P("dom", "blk", None, None, None, None),
            P("dom", "blk", None),
            P("dom", "blk"),
            P("dom", None, None, "blk"),
            P("dom", None, None, "blk"),
            P("dom", "blk", None, None, None, None),
            P("dom", "blk", None),
        ),
        out_specs=(P(None, None, "dom", "blk"), P(None, None, "dom", "blk"), P()),
        check_vma=False,
    )
```

profile of v0, /device:TPU:0, one launch (start us, length us, event | category | flops | bytes accessed | tf_op | source)
XLA Modules:
  0.0 278.6 jit_solution(17837477689193010791)
XLA Ops:
  0.7 1.0 add_reduce_fusion.3
  1.7 42.0 %psum.35 = f32[4]{0:T(128)S(1)} all-reduce(f32[4]{0:T(128)S(1)} %add_reduce_fusion.3), channel_id=1, replica_groups=mesh['dom'=2,'blk'=16] {'dom','blk'}, use_global_device_ids=true, to_apply=%region_1.0 | all-reduce | flops 4 | bytes 32 | tf_op jit(solution)/shard_map/psum | solution.py:107
  43.7 0.8 fusion.64
  44.5 1.3 collective-permute-start
  45.8 1.3 collective-permute-start.1
  47.1 1.1 convolution_bitcast_fusion.3
  48.2 24.1 %all-gather = f32[32,4,64]{2,1,0:T(4,128)S(1)} all-gather(f32[2,4,64]{2,1,0:T(4,128)S(1)} %pad_maximum_fusion.2), channel_id=2, replica_groups=mesh['dom'=2,'blk'=16] {'blk'}, dimensions={0}, use_global_device_ids=true | all-gather | bytes 34816 | tf_op jit(solution)/shard_map/all_gather | solution.py:62
  72.3 0.7 iota_compare_fusion
  73.0 0.2 and_convert_fusion
  73.2 2.6 fusion.12
  75.9 0.1 convolution_bitcast_fusion.1
  76.1 0.1 reshape_squeeze.4
  76.2 4.4 %all_gather.13 = f32[2,4,2,512]{3,1,0,2:T(4,128)S(1)} all-gather(f32[2,4,1,512]{3,1,0,2:T(4,128)S(1)} %get-tuple-element.28), channel_id=1, replica_groups=mesh['dom'=2,'blk'=16] {'dom'}, dimensions={2}, use_global_device_ids=true | all-gather | bytes 49152 | tf_op jit(solution)/shard_map/all_gather | solution.py:71
  80.7 0.6 gather_fusion.1
  81.5 0.6 gather_fusion
  82.1 0.1 broadcast_select_fusion.1
  82.2 0.7 fusion.4
  82.9 0.1 add_reduce_fusion.2
  83.1 36.9 %psum.36 = f32[1,2,4]{2,1,0:T(2,128)S(1)} all-reduce(f32[1,2,4]{2,1,0:T(2,128)S(1)} %maximum_bitcast_fusion.6), channel_id=1, replica_groups=mesh['dom'=2,'blk'=16] {'dom','blk'}, use_global_device_ids=true, to_apply=%region_4.7 | all-reduce | flops 8 | bytes 64 | tf_op jit(solution)/shard_map/psum | solution.py:113
  120.1 0.1 fusion.34
  120.2 0.1 copy.136
  120.3 41.3 %psum.37 = f32[4]{0:T(128)S(1)} all-reduce(f32[4]{0:T(128)S(1)} %fusion.34), channel_id=1, replica_groups=mesh['dom'=2,'blk'=16] {'dom','blk'}, use_global_device_ids=true, to_apply=%region_6.9 | all-reduce | flops 4 | bytes 32 | tf_op jit(solution)/shard_map/psum | solution.py:116
  161.7 0.1 convolution_bitcast_fusion.2
  161.9 20.6 %all-gather.1 = f32[32,4,64]{2,1,0:T(4,128)S(1)} all-gather(f32[2,4,64]{2,1,0:T(4,128)S(1)} %pad_maximum_fusion.3), channel_id=3, replica_groups=mesh['dom'=2,'blk'=16] {'blk'}, dimensions={0}, use_global_device_ids=true | all-gather | bytes 34816 | tf_op jit(solution)/shard_map/all_gather | solution.py:62
  182.5 2.6 fusion.10
  185.1 2.2 collective-permute-start.2
  187.4 1.3 collective-permute-start.3
  188.7 4.4 %all_gather.15 = f32[2,4,2,512]{3,1,0,2:T(4,128)S(1)} all-gather(f32[2,4,1,512]{3,1,0,2:T(4,128)S(1)} %get-tuple-element.26), channel_id=1, replica_groups=mesh['dom'=2,'blk'=16] {'dom'}, dimensions={2}, use_global_device_ids=true | all-gather | bytes 49152 | tf_op jit(solution)/shard_map/all_gather | solution.py:71
  193.2 0.6 gather_fusion.3
  193.9 0.1 convolution_bitcast_fusion
  194.0 0.6 copy.145
  194.7 0.1 copy.139
  194.8 0.6 gather_fusion.2
  195.4 0.1 broadcast_select_fusion
  195.5 0.7 fusion.7
  196.2 0.2 add_reduce_fusion.1
  196.4 0.1 copy.137
  196.5 39.3 %psum.38 = f32[2,2,4]{2,1,0:T(2,128)S(1)} all-reduce(f32[2,2,4]{2,1,0:T(2,128)S(1)} %pad_maximum_fusion.4), channel_id=1, replica_groups=mesh['dom'=2,'blk'=16] {'dom','blk'}, use_global_device_ids=true, to_apply=%region_11.14 | all-reduce | flops 16 | bytes 128 | tf_op jit(solution)/shard_map/psum | solution.py:113
  236.0 0.1 fusion.30
  236.1 0.1 copy.138
  236.2 40.5 %psum.39 = f32[4]{0:T(128)S(1)} all-reduce(f32[4]{0:T(128)S(1)} %fusion.30), channel_id=1, replica_groups=mesh['dom'=2,'blk'=16] {'dom','blk'}, use_global_device_ids=true, to_apply=%region_13.16 | all-reduce | flops 4 | bytes 32 | tf_op jit(solution)/shard_map/psum | solution.py:116
  276.7 0.1 copy.144
  276.8 0.1 copy.140
  276.9 0.1 copy.141
  277.0 0.1 copy.142
  277.1 0.1 copy.143
  277.3 0.6 copy.146
  277.9 0.7 stack.135
  (72 shorter events, 1.1 us)
Async XLA Ops:
  0.6 81.5 %copy-start = (bf16[1,2,4,2,256,256]{5,4,3,2,1,0:T(8,128)(2,1)S(1)}, bf16[1,2,4,2,256,256]{5,4,3,2,1,0:T(8,128)(2,1)}, u32[]{:S(2)}) copy-start(bf16[1,2,4,2,256,256]{5,4,3,2,1,0:T(8,128)(2,1)} %param.13) | copy-start | bytes 6291460
  0.6 75.3 %copy-start.2 = (bf16[1,2,64,512]{3,2,1,0:T(8,128)(2,1)S(1)}, bf16[1,2,64,512]{3,2,1,0:T(8,128)(2,1)}, u32[]{:S(2)}) copy-start(bf16[1,2,64,512]{3,2,1,0:T(8,128)(2,1)} %param.17) | copy-start | bytes 393220
  0.7 75.4 %copy-start.3 = (s32[1,2,4]{2,1,0:T(2,128)S(1)}, s32[1,2,4]{2,1,0:T(2,128)}, u32[]{:S(2)}) copy-start(s32[1,2,4]{2,1,0:T(2,128)} %param.14) | copy-start | bytes 100
  0.7 75.5 %copy-start.4 = (s32[1,2]{1,0:T(1,128)S(1)}, s32[1,2]{1,0:T(1,128)}, u32[]{:S(2)}) copy-start(s32[1,2]{1,0:T(1,128)} %param.15) | copy-start | bytes 28
  44.5 37.0 %collective-permute-start = (bf16[2,4,1,512]{3,1,0,2:T(4,128)(2,1)S(1)}, bf16[2,4,1,512]{3,1,0,2:T(4,128)(2,1)S(1)}, u32[]{:S(2)}, u32[]{:S(2)}) collective-permute-start(bf16[2,4,1,512]{3,1,0,2:T(4,128)(2,1)S(1)} %get-tuple-element.27), channel_id=1, source_target_pairs={{0,1},{1,2},{2,3},{3,4},{4,5},{5,6},{6,7},{7,8},{8,9},{9,10},{10,1... | collective-permute-start | bytes 24584 | tf_op jit(solution)/shard_map/ppermute | solution.py:17
  45.8 35.7 %collective-permute-start.1 = (bf16[2,4,1,512]{3,1,0,2:T(4,128)(2,1)S(1)}, bf16[2,4,1,512]{3,1,0,2:T(4,128)(2,1)S(1)}, u32[]{:S(2)}, u32[]{:S(2)}) collective-permute-start(bf16[2,4,1,512]{3,1,0,2:T(4,128)(2,1)S(1)} %get-tuple-element.27), channel_id=1, source_target_pairs={{1,0},{2,1},{3,2},{4,3},{5,4},{6,5},{7,6},{8,7},{9,8},{10,9},{11,1... | collective-permute-start | bytes 24584 | tf_op jit(solution)/shard_map/ppermute | solution.py:19
  75.9 85.8 %copy-start.1 = (bf16[1,2,64,512]{3,2,1,0:T(8,128)(2,1)S(1)}, bf16[1,2,64,512]{3,2,1,0:T(8,128)(2,1)}, u32[]{:S(2)}) copy-start(bf16[1,2,64,512]{3,2,1,0:T(8,128)(2,1)} %param.16) | copy-start | bytes 393220
  185.1 9.7 %collective-permute-start.2 = (bf16[2,4,1,512]{3,1,0,2:T(4,128)(2,1)S(1)}, bf16[2,4,1,512]{3,1,0,2:T(4,128)(2,1)S(1)}, u32[]{:S(2)}, u32[]{:S(2)}) collective-permute-start(bf16[2,4,1,512]{3,1,0,2:T(4,128)(2,1)S(1)} %get-tuple-element.25), channel_id=1, source_target_pairs={{0,1},{1,2},{2,3},{3,4},{4,5},{5,6},{6,7},{7,8},{8,9},{9,10},{10,1... | collective-permute-start | bytes 24584 | tf_op jit(solution)/shard_map/ppermute | solution.py:17
  187.4 7.4 %collective-permute-start.3 = (bf16[2,4,1,512]{3,1,0,2:T(4,128)(2,1)S(1)}, bf16[2,4,1,512]{3,1,0,2:T(4,128)(2,1)S(1)}, u32[]{:S(2)}, u32[]{:S(2)}) collective-permute-start(bf16[2,4,1,512]{3,1,0,2:T(4,128)(2,1)S(1)} %get-tuple-element.25), channel_id=1, source_target_pairs={{1,0},{2,1},{3,2},{4,3},{5,4},{6,5},{7,6},{8,7},{9,8},{10,9},{11,1... | collective-permute-start | bytes 24584 | tf_op jit(solution)/shard_map/ppermute | solution.py:19
where the time goes:
time: 280 us; the launch traced here: 279 us
  blocking collectives  254 us (91%)
  matrix products  8.05 us (3%)
  starting transfers between devices  6.11 us (2%)
  local copies, waits for them, and re-layouts  5.44 us (2%)
  other arithmetic  4.26 us (2%)
    psum x2, blocking collectives, lengths(): return lax.psum(local_squares(field), ('dom', 'blk')) / total  81.9 us
    psum x2, blocking collectives, projections(): return lax.psum(local_products(vectors, image), ('dom', 'blk')) / total  76.2 us
    all_gather x2, blocking collectives, apply_operator(): lax.all_gather(coeffs[None], 'blk', axis=0, tiled=True)  44.7 us
    psum x1, blocking collectives, shards(): start_sum = lax.psum(local_squares(right_side), ('dom', 'blk'))  42 us
    all_gather x2, blocking collectives, apply_operator(): every = lax.all_gather(vector, 'dom', axis=2, tiled=True)  8.85 us
  transfers between devices with their start and end apart: 4, of which 0 were waited for; matrix products, arithmetic and copies ran while one was open for 3% of the time, Pallas kernels for 0%

commit v1 on v0

--- a/solution.py
+++ b/solution.py
@@ -56,12 +56,27 @@
     limit = row_ranks[:, None, None]
     keep = (levels[None, :, None] < limit) & (levels[None, None, :] < limit)
     weights = row_coupling * keep[:, None].astype(jnp.float32)
-    inner = jnp.einsum(
+    count_2, index = (lax.axis_size("blk"), lax.axis_index("blk"))
+    behind = [(i_2, (i_2 - 1) % count_2) for i_2 in range(count_2)]
+    rows_2 = coeffs[None].shape[0]
+    carried = coeffs[None]
+    running = jnp.einsum(
         "sakl,spql->apqk",
-        weights,
-        lax.all_gather(coeffs[None], "blk", axis=0, tiled=True),
+        lax.dynamic_slice_in_dim(weights, index * rows_2, carried.shape[0], axis=0),
+        carried,
         precision=lax.Precision.HIGHEST,
     )
+    for lap in range(1, count_2):
+        carried = lax.ppermute(carried, "blk", behind)
+        running = running + jnp.einsum(
+            "sakl,spql->apqk",
+            lax.dynamic_slice_in_dim(
+                weights, (index + lap) % count_2 * rows_2, carried.shape[0], axis=0
+            ),
+            carried,
+            precision=lax.Precision.HIGHEST,
+        )
+    inner = running
     far_coef = complex_mix(inner)
     rounded_coef = far_coef.astype(jnp.bfloat16)
     outward = jnp.einsum(

time: 280 us -> 395 us (1.41)
  starting transfers between devices: 6.11 us -> 130 us
  blocking collectives: 254 us -> 210 us
  waiting for transfers between devices: 0.01 us -> 27.9 us
    ppermute x0 -> x30, starting transfers between devices: none -> 124 us  [apply_operator(): carried = lax.ppermute(carried, 'blk', behind)]
    all_gather x2 -> x0, blocking collectives: 44.7 us -> none  [apply_operator(): lax.all_gather(coeffs[None], 'blk', axis=0, tiled=True)]
    ppermute x0 -> x30, waiting for transfers between devices: none -> 27.9 us  [apply_operator(): carried = lax.ppermute(carried, 'blk', behind)]
    dot_general x2 -> x32, matrix products: 5.25 us -> 8.14 us  [the longest x30 7.63 us: apply_operator(): jnp.einsum('sakl,spql->apqk', lax.dynamic_slice_in_dim(weights, (index +...]
  transfers between devices with their start and end apart: 4 -> 34, of which waited for: 0 -> 26; matrix products, arithmetic and copies ran while one was open for 3% -> 5% of each run, Pallas kernels for 0% -> 0%
where the time goes in v1:
time: 395 us; the launch traced here: 394 us
  blocking collectives  210 us (53%)
  starting transfers between devices  130 us (33%)
  waiting for transfers between devices  27.9 us (7%)
  matrix products  10.9 us (3%)
  other arithmetic  7.86 us (2%)
  local copies, waits for them, and re-layouts  6.14 us (2%)
    ppermute x30, starting transfers between devices, apply_operator(): carried = lax.ppermute(carried, 'blk', behind)  124 us
    psum x2, blocking collectives, lengths(): return lax.psum(local_squares(field), ('dom', 'blk')) / total  82.1 us
    psum x2, blocking collectives, projections(): return lax.psum(local_products(vectors, image), ('dom', 'blk')) / total  77.4 us
    psum x1, blocking collectives, shards(): start_sum = lax.psum(local_squares(right_side), ('dom', 'blk'))  42 us
    ppermute x30, waiting for transfers between devices, apply_operator(): carried = lax.ppermute(carried, 'blk', behind)  27.9 us
    all_gather x2, blocking collectives, apply_operator(): every = lax.all_gather(vector, 'dom', axis=2, tiled=True)  8.81 us
  transfers between devices with their start and end apart: 34, of which 26 were waited for; matrix products, arithmetic and copies ran while one was open for 5% of the time, Pallas kernels for 0%

profile of v1, /device:TPU:0, one launch (start us, length us, event | category | flops | bytes accessed | tf_op | source)
XLA Modules:
  0.0 393.9 jit_solution(4930439934897269310)
XLA Ops:
  1.6 42.0 %psum.35 = f32[4]{0:T(128)S(1)} all-reduce(f32[4]{0:T(128)S(1)} %add_reduce_fusion.3), channel_id=1, replica_groups=mesh['dom'=2,'blk'=16] {'dom','blk'}, use_global_device_ids=true, to_apply=%region_1.0 | all-reduce | flops 4 | bytes 32 | tf_op jit(solution)/shard_map/psum | solution.py:122
  44.4 1.3 collective-permute-start
  45.7 1.3 collective-permute-start.1
  48.1 5.3 %collective-permute-start.2 = (f32[1,2,4,64]{3,2,1,0:T(4,128)S(1)}, f32[1,2,4,64]{3,2,1,0:T(4,128)S(1)}, u32[]{:S(2)}, u32[]{:S(2)}) collective-permute-start(f32[1,2,4,64]{3,2,1,0:T(4,128)S(1)} %fusion.165), channel_id=1, source_target_pairs={{0,15},{1,0},{2,1},{3,2},{4,3},{5,4},{6,5},{7,6},{8,7},{9,8},{10,9... | collective-permute-start | bytes 6152 | tf_op jit(solution)/shard_map/ppermute | solution.py:70
  57.3 4.4 %all_gather.6 = f32[2,4,2,512]{3,1,0,2:T(4,128)S(1)} all-gather(f32[2,4,1,512]{3,1,0,2:T(4,128)S(1)} %get-tuple-element.25), channel_id=1, replica_groups=mesh['dom'=2,'blk'=16] {'dom'}, dimensions={2}, use_global_device_ids=true | all-gather | bytes 49152 | tf_op jit(solution)/shard_map/all_gather | solution.py:86
  61.8 1.5 bitcast_multiply_fusion
  66.3 4.4 %collective-permute-start.4 = (f32[1,2,4,64]{3,2,1,0:T(4,128)S(1)}, f32[1,2,4,64]{3,2,1,0:T(4,128)S(1)}, u32[]{:S(2)}, u32[]{:S(2)}) collective-permute-start(f32[1,2,4,64]{3,2,1,0:T(4,128)S(1)} %collective-permute-done.3), channel_id=1, source_target_pairs={{0,15},{1,0},{2,1},{3,2},{4,3},{5,4},{6,5},{7,6},{8,7},{9,8},{10,9... | collective-permute-start | bytes 6152 | tf_op jit(solution)/shard_map/ppermute | solution.py:70
  71.0 1.1 collective-permute-done.4
  72.0 4.4 %collective-permute-start.5 = (f32[1,2,4,64]{3,2,1,0:T(4,128)S(1)}, f32[1,2,4,64]{3,2,1,0:T(4,128)S(1)}, u32[]{:S(2)}, u32[]{:S(2)}) collective-permute-start(f32[1,2,4,64]{3,2,1,0:T(4,128)S(1)} %collective-permute-done.4), channel_id=1, source_target_pairs={{0,15},{1,0},{2,1},{3,2},{4,3},{5,4},{6,5},{7,6},{8,7},{9,8},{10,9... | collective-permute-start | bytes 6152 | tf_op jit(solution)/shard_map/ppermute | solution.py:70
  78.1 4.0 %collective-permute-start.6 = (f32[1,2,4,64]{3,2,1,0:T(4,128)S(1)}, f32[1,2,4,64]{3,2,1,0:T(4,128)S(1)}, u32[]{:S(2)}, u32[]{:S(2)}) collective-permute-start(f32[1,2,4,64]{3,2,1,0:T(4,128)S(1)} %collective-permute-done.5), channel_id=1, source_target_pairs={{0,15},{1,0},{2,1},{3,2},{4,3},{5,4},{6,5},{7,6},{8,7},{9,8},{10,9... | collective-permute-start | bytes 6152 | tf_op jit(solution)/shard_map/ppermute | solution.py:70
  82.4 1.1 collective-permute-done.6
  83.5 4.4 %collective-permute-start.7 = (f32[1,2,4,64]{3,2,1,0:T(4,128)S(1)}, f32[1,2,4,64]{3,2,1,0:T(4,128)S(1)}, u32[]{:S(2)}, u32[]{:S(2)}) collective-permute-start(f32[1,2,4,64]{3,2,1,0:T(4,128)S(1)} %collective-permute-done.6), channel_id=1, source_target_pairs={{0,15},{1,0},{2,1},{3,2},{4,3},{5,4},{6,5},{7,6},{8,7},{9,8},{10,9... | collective-permute-start | bytes 6152 | tf_op jit(solution)/shard_map/ppermute | solution.py:70
  88.1 1.1 collective-permute-done.7
  89.2 4.4 %collective-permute-start.8 = (f32[1,2,4,64]{3,2,1,0:T(4,128)S(1)}, f32[1,2,4,64]{3,2,1,0:T(4,128)S(1)}, u32[]{:S(2)}, u32[]{:S(2)}) collective-permute-start(f32[1,2,4,64]{3,2,1,0:T(4,128)S(1)} %collective-permute-done.7), channel_id=1, source_target_pairs={{0,15},{1,0},{2,1},{3,2},{4,3},{5,4},{6,5},{7,6},{8,7},{9,8},{10,9... | collective-permute-start | bytes 6152 | tf_op jit(solution)/shard_map/ppermute | solution.py:70
  93.9 1.1 collective-permute-done.8
  95.0 4.4 %collective-permute-start.9 = (f32[1,2,4,64]{3,2,1,0:T(4,128)S(1)}, f32[1,2,4,64]{3,2,1,0:T(4,128)S(1)}, u32[]{:S(2)}, u32[]{:S(2)}) collective-permute-start(f32[1,2,4,64]{3,2,1,0:T(4,128)S(1)} %collective-permute-done.8), channel_id=1, source_target_pairs={{0,15},{1,0},{2,1},{3,2},{4,3},{5,4},{6,5},{7,6},{8,7},{9,8},{10,9... | collective-permute-start | bytes 6152 | tf_op jit(solution)/shard_map/ppermute | solution.py:70
  99.6 1.1 collective-permute-done.9
  100.7 4.4 %collective-permute-start.10 = (f32[1,2,4,64]{3,2,1,0:T(4,128)S(1)}, f32[1,2,4,64]{3,2,1,0:T(4,128)S(1)}, u32[]{:S(2)}, u32[]{:S(2)}) collective-permute-start(f32[1,2,4,64]{3,2,1,0:T(4,128)S(1)} %collective-permute-done.9), channel_id=1, source_target_pairs={{0,15},{1,0},{2,1},{3,2},{4,3},{5,4},{6,5},{7,6},{8,7},{9,8},{10,9... | collective-permute-start | bytes 6152 | tf_op jit(solution)/shard_map/ppermute | solution.py:70
  105.3 1.1 collective-permute-done.10
  106.4 4.4 %collective-permute-start.11 = (f32[1,2,4,64]{3,2,1,0:T(4,128)S(1)}, f32[1,2,4,64]{3,2,1,0:T(4,128)S(1)}, u32[]{:S(2)}, u32[]{:S(2)}) collective-permute-start(f32[1,2,4,64]{3,2,1,0:T(4,128)S(1)} %collective-permute-done.10), channel_id=1, source_target_pairs={{0,15},{1,0},{2,1},{3,2},{4,3},{5,4},{6,5},{7,6},{8,7},{9,8},{10,9... | collective-permute-start | bytes 6152 | tf_op jit(solution)/shard_map/ppermute | solution.py:70
  111.1 1.1 collective-permute-done.11
  112.1 4.4 %collective-permute-start.12 = (f32[1,2,4,64]{3,2,1,0:T(4,128)S(1)}, f32[1,2,4,64]{3,2,1,0:T(4,128)S(1)}, u32[]{:S(2)}, u32[]{:S(2)}) collective-permute-start(f32[1,2,4,64]{3,2,1,0:T(4,128)S(1)} %collective-permute-done.11), channel_id=1, source_target_pairs={{0,15},{1,0},{2,1},{3,2},{4,3},{5,4},{6,5},{7,6},{8,7},{9,8},{10,9... | collective-permute-start | bytes 6152 | tf_op jit(solution)/shard_map/ppermute | solution.py:70
  116.8 1.1 collective-permute-done.12
  117.9 4.4 %collective-permute-start.13 = (f32[1,2,4,64]{3,2,1,0:T(4,128)S(1)}, f32[1,2,4,64]{3,2,1,0:T(4,128)S(1)}, u32[]{:S(2)}, u32[]{:S(2)}) collective-permute-start(f32[1,2,4,64]{3,2,1,0:T(4,128)S(1)} %collective-permute-done.12), channel_id=1, source_target_pairs={{0,15},{1,0},{2,1},{3,2},{4,3},{5,4},{6,5},{7,6},{8,7},{9,8},{10,9... | collective-permute-start | bytes 6152 | tf_op jit(solution)/shard_map/ppermute | solution.py:70
  123.6 4.4 %collective-permute-start.14 = (f32[1,2,4,64]{3,2,1,0:T(4,128)S(1)}, f32[1,2,4,64]{3,2,1,0:T(4,128)S(1)}, u32[]{:S(2)}, u32[]{:S(2)}) collective-permute-start(f32[1,2,4,64]{3,2,1,0:T(4,128)S(1)} %collective-permute-done.13), channel_id=1, source_target_pairs={{0,15},{1,0},{2,1},{3,2},{4,3},{5,4},{6,5},{7,6},{8,7},{9,8},{10,9... | collective-permute-start | bytes 6152 | tf_op jit(solution)/shard_map/ppermute | solution.py:70
  129.3 4.4 %collective-permute-start.15 = (f32[1,2,4,64]{3,2,1,0:T(4,128)S(1)}, f32[1,2,4,64]{3,2,1,0:T(4,128)S(1)}, u32[]{:S(2)}, u32[]{:S(2)}) collective-permute-start(f32[1,2,4,64]{3,2,1,0:T(4,128)S(1)} %collective-permute-done.14), channel_id=1, source_target_pairs={{0,15},{1,0},{2,1},{3,2},{4,3},{5,4},{6,5},{7,6},{8,7},{9,8},{10,9... | collective-permute-start | bytes 6152 | tf_op jit(solution)/shard_map/ppermute | solution.py:70
  135.1 4.4 %collective-permute-start.16 = (f32[1,2,4,64]{3,2,1,0:T(4,128)S(1)}, f32[1,2,4,64]{3,2,1,0:T(4,128)S(1)}, u32[]{:S(2)}, u32[]{:S(2)}) collective-permute-start(f32[1,2,4,64]{3,2,1,0:T(4,128)S(1)} %collective-permute-done.15), channel_id=1, source_target_pairs={{0,15},{1,0},{2,1},{3,2},{4,3},{5,4},{6,5},{7,6},{8,7},{9,8},{10,9... | collective-permute-start | bytes 6152 | tf_op jit(solution)/shard_map/ppermute | solution.py:70
  141.4 38.7 %psum.36 = f32[1,2,4]{2,1,0:T(2,128)S(1)} all-reduce(f32[1,2,4]{2,1,0:T(2,128)S(1)} %maximum_bitcast_fusion.6), channel_id=1, replica_groups=mesh['dom'=2,'blk'=16] {'dom','blk'}, use_global_device_ids=true, to_apply=%region_4.7 | all-reduce | flops 8 | bytes 64 | tf_op jit(solution)/shard_map/psum | solution.py:128
  180.4 40.7 %psum.37 = f32[4]{0:T(128)S(1)} all-reduce(f32[4]{0:T(128)S(1)} %fusion.94), channel_id=1, replica_groups=mesh['dom'=2,'blk'=16] {'dom','blk'}, use_global_device_ids=true, to_apply=%region_6.9 | all-reduce | flops 4 | bytes 32 | tf_op jit(solution)/shard_map/psum | solution.py:131
  221.4 1.3 collective-permute-start.18
  222.7 4.7 %collective-permute-start.19 = (f32[1,2,4,64]{3,2,1,0:T(4,128)S(1)}, f32[1,2,4,64]{3,2,1,0:T(4,128)S(1)}, u32[]{:S(2)}, u32[]{:S(2)}) collective-permute-start(f32[1,2,4,64]{3,2,1,0:T(4,128)S(1)} %fusion.164), channel_id=1, source_target_pairs={{0,15},{1,0},{2,1},{3,2},{4,3},{5,4},{6,5},{7,6},{8,7},{9,8},{10,9... | collective-permute-start | bytes 6152 | tf_op jit(solution)/shard_map/ppermute | solution.py:70
  227.4 4.4 %all_gather.7 = f32[2,4,2,512]{3,1,0,2:T(4,128)S(1)} all-gather(f32[2,4,1,512]{3,1,0,2:T(4,128)S(1)} %get-tuple-element.23), channel_id=1, replica_groups=mesh['dom'=2,'blk'=16] {'dom'}, dimensions={2}, use_global_device_ids=true | all-gather | bytes 49152 | tf_op jit(solution)/shard_map/all_gather | solution.py:86
  232.8 1.3 collective-permute-start.17
  236.2 4.4 %collective-permute-start.21 = (f32[1,2,4,64]{3,2,1,0:T(4,128)S(1)}, f32[1,2,4,64]{3,2,1,0:T(4,128)S(1)}, u32[]{:S(2)}, u32[]{:S(2)}) collective-permute-start(f32[1,2,4,64]{3,2,1,0:T(4,128)S(1)} %collective-permute-done.20), channel_id=1, source_target_pairs={{0,15},{1,0},{2,1},{3,2},{4,3},{5,4},{6,5},{7,6},{8,7},{9,8},{10,9... | collective-permute-start | bytes 6152 | tf_op jit(solution)/shard_map/ppermute | solution.py:70
  242.0 4.4 %collective-permute-start.22 = (f32[1,2,4,64]{3,2,1,0:T(4,128)S(1)}, f32[1,2,4,64]{3,2,1,0:T(4,128)S(1)}, u32[]{:S(2)}, u32[]{:S(2)}) collective-permute-start(f32[1,2,4,64]{3,2,1,0:T(4,128)S(1)} %collective-permute-done.21), channel_id=1, source_target_pairs={{0,15},{1,0},{2,1},{3,2},{4,3},{5,4},{6,5},{7,6},{8,7},{9,8},{10,9... | collective-permute-start | bytes 6152 | tf_op jit(solution)/shard_map/ppermute | solution.py:70
  248.1 4.0 %collective-permute-start.23 = (f32[1,2,4,64]{3,2,1,0:T(4,128)S(1)}, f32[1,2,4,64]{3,2,1,0:T(4,128)S(1)}, u32[]{:S(2)}, u32[]{:S(2)}) collective-permute-start(f32[1,2,4,64]{3,2,1,0:T(4,128)S(1)} %collective-permute-done.22), channel_id=1, source_target_pairs={{0,15},{1,0},{2,1},{3,2},{4,3},{5,4},{6,5},{7,6},{8,7},{9,8},{10,9... | collective-permute-start | bytes 6152 | tf_op jit(solution)/shard_map/ppermute | solution.py:70
  253.4 4.4 %collective-permute-start.24 = (f32[1,2,4,64]{3,2,1,0:T(4,128)S(1)}, f32[1,2,4,64]{3,2,1,0:T(4,128)S(1)}, u32[]{:S(2)}, u32[]{:S(2)}) collective-permute-start(f32[1,2,4,64]{3,2,1,0:T(4,128)S(1)} %collective-permute-done.23), channel_id=1, source_target_pairs={{0,15},{1,0},{2,1},{3,2},{4,3},{5,4},{6,5},{7,6},{8,7},{9,8},{10,9... | collective-permute-start | bytes 6152 | tf_op jit(solution)/shard_map/ppermute | solution.py:70
  259.2 4.4 %collective-permute-start.25 = (f32[1,2,4,64]{3,2,1,0:T(4,128)S(1)}, f32[1,2,4,64]{3,2,1,0:T(4,128)S(1)}, u32[]{:S(2)}, u32[]{:S(2)}) collective-permute-start(f32[1,2,4,64]{3,2,1,0:T(4,128)S(1)} %collective-permute-done.24), channel_id=1, source_target_pairs={{0,15},{1,0},{2,1},{3,2},{4,3},{5,4},{6,5},{7,6},{8,7},{9,8},{10,9... | collective-permute-start | bytes 6152 | tf_op jit(solution)/shard_map/ppermute | solution.py:70
  264.9 4.4 %collective-permute-start.26 = (f32[1,2,4,64]{3,2,1,0:T(4,128)S(1)}, f32[1,2,4,64]{3,2,1,0:T(4,128)S(1)}, u32[]{:S(2)}, u32[]{:S(2)}) collective-permute-start(f32[1,2,4,64]{3,2,1,0:T(4,128)S(1)} %collective-permute-done.25), channel_id=1, source_target_pairs={{0,15},{1,0},{2,1},{3,2},{4,3},{5,4},{6,5},{7,6},{8,7},{9,8},{10,9... | collective-permute-start | bytes 6152 | tf_op jit(solution)/shard_map/ppermute | solution.py:70
  270.6 4.4 %collective-permute-start.27 = (f32[1,2,4,64]{3,2,1,0:T(4,128)S(1)}, f32[1,2,4,64]{3,2,1,0:T(4,128)S(1)}, u32[]{:S(2)}, u32[]{:S(2)}) collective-permute-start(f32[1,2,4,64]{3,2,1,0:T(4,128)S(1)} %collective-permute-done.26), channel_id=1, source_target_pairs={{0,15},{1,0},{2,1},{3,2},{4,3},{5,4},{6,5},{7,6},{8,7},{9,8},{10,9... | collective-permute-start | bytes 6152 | tf_op jit(solution)/shard_map/ppermute | solution.py:70
  276.4 4.4 %collective-permute-start.28 = (f32[1,2,4,64]{3,2,1,0:T(4,128)S(1)}, f32[1,2,4,64]{3,2,1,0:T(4,128)S(1)}, u32[]{:S(2)}, u32[]{:S(2)}) collective-permute-start(f32[1,2,4,64]{3,2,1,0:T(4,128)S(1)} %collective-permute-done.27), channel_id=1, source_target_pairs={{0,15},{1,0},{2,1},{3,2},{4,3},{5,4},{6,5},{7,6},{8,7},{9,8},{10,9... | collective-permute-start | bytes 6152 | tf_op jit(solution)/shard_map/ppermute | solution.py:70
  282.1 4.4 %collective-permute-start.29 = (f32[1,2,4,64]{3,2,1,0:T(4,128)S(1)}, f32[1,2,4,64]{3,2,1,0:T(4,128)S(1)}, u32[]{:S(2)}, u32[]{:S(2)}) collective-permute-start(f32[1,2,4,64]{3,2,1,0:T(4,128)S(1)} %collective-permute-done.28), channel_id=1, source_target_pairs={{0,15},{1,0},{2,1},{3,2},{4,3},{5,4},{6,5},{7,6},{8,7},{9,8},{10,9... | collective-permute-start | bytes 6152 | tf_op jit(solution)/shard_map/ppermute | solution.py:70
  287.8 4.4 %collective-permute-start.30 = (f32[1,2,4,64]{3,2,1,0:T(4,128)S(1)}, f32[1,2,4,64]{3,2,1,0:T(4,128)S(1)}, u32[]{:S(2)}, u32[]{:S(2)}) collective-permute-start(f32[1,2,4,64]{3,2,1,0:T(4,128)S(1)} %collective-permute-done.29), channel_id=1, source_target_pairs={{0,15},{1,0},{2,1},{3,2},{4,3},{5,4},{6,5},{7,6},{8,7},{9,8},{10,9... | collective-permute-start | bytes 6152 | tf_op jit(solution)/shard_map/ppermute | solution.py:70
  293.5 4.4 %collective-permute-start.31 = (f32[1,2,4,64]{3,2,1,0:T(4,128)S(1)}, f32[1,2,4,64]{3,2,1,0:T(4,128)S(1)}, u32[]{:S(2)}, u32[]{:S(2)}) collective-permute-start(f32[1,2,4,64]{3,2,1,0:T(4,128)S(1)} %collective-permute-done.30), channel_id=1, source_target_pairs={{0,15},{1,0},{2,1},{3,2},{4,3},{5,4},{6,5},{7,6},{8,7},{9,8},{10,9... | collective-permute-start | bytes 6152 | tf_op jit(solution)/shard_map/ppermute | solution.py:70
  299.3 4.4 %collective-permute-start.32 = (f32[1,2,4,64]{3,2,1,0:T(4,128)S(1)}, f32[1,2,4,64]{3,2,1,0:T(4,128)S(1)}, u32[]{:S(2)}, u32[]{:S(2)}) collective-permute-start(f32[1,2,4,64]{3,2,1,0:T(4,128)S(1)} %collective-permute-done.31), channel_id=1, source_target_pairs={{0,15},{1,0},{2,1},{3,2},{4,3},{5,4},{6,5},{7,6},{8,7},{9,8},{10,9... | collective-permute-start | bytes 6152 | tf_op jit(solution)/shard_map/ppermute | solution.py:70
  305.0 4.4 %collective-permute-start.33 = (f32[1,2,4,64]{3,2,1,0:T(4,128)S(1)}, f32[1,2,4,64]{3,2,1,0:T(4,128)S(1)}, u32[]{:S(2)}, u32[]{:S(2)}) collective-permute-start(f32[1,2,4,64]{3,2,1,0:T(4,128)S(1)} %collective-permute-done.32), channel_id=1, source_target_pairs={{0,15},{1,0},{2,1},{3,2},{4,3},{5,4},{6,5},{7,6},{8,7},{9,8},{10,9... | collective-permute-start | bytes 6152 | tf_op jit(solution)/shard_map/ppermute | solution.py:70
  311.5 38.7 %psum.38 = f32[2,2,4]{2,1,0:T(2,128)S(1)} all-reduce(f32[2,2,4]{2,1,0:T(2,128)S(1)} %pad_maximum_fusion.6), channel_id=1, replica_groups=mesh['dom'=2,'blk'=16] {'dom','blk'}, use_global_device_ids=true, to_apply=%region_11.14 | all-reduce | flops 16 | bytes 128 | tf_op jit(solution)/shard_map/psum | solution.py:128
  350.6 41.4 %psum.39 = f32[4]{0:T(128)S(1)} all-reduce(f32[4]{0:T(128)S(1)} %fusion.90), channel_id=1, replica_groups=mesh['dom'=2,'blk'=16] {'dom','blk'}, use_global_device_ids=true, to_apply=%region_13.16 | all-reduce | flops 4 | bytes 32 | tf_op jit(solution)/shard_map/psum | solution.py:131
  (153 shorter events, 43.5 us)
Async XLA Ops:
  0.6 76.8 %copy-start = (bf16[1,2,4,2,256,256]{5,4,3,2,1,0:T(8,128)(2,1)S(1)}, bf16[1,2,4,2,256,256]{5,4,3,2,1,0:T(8,128)(2,1)}, u32[]{:S(2)}) copy-start(bf16[1,2,4,2,256,256]{5,4,3,2,1,0:T(8,128)(2,1)} %param.13) | copy-start | bytes 6291460
  44.4 32.3 %collective-permute-start = (bf16[2,4,1,512]{3,1,0,2:T(4,128)(2,1)S(1)}, bf16[2,4,1,512]{3,1,0,2:T(4,128)(2,1)S(1)}, u32[]{:S(2)}, u32[]{:S(2)}) collective-permute-start(bf16[2,4,1,512]{3,1,0,2:T(4,128)(2,1)S(1)} %get-tuple-element.24), channel_id=1, source_target_pairs={{0,1},{1,2},{2,3},{3,4},{4,5},{5,6},{6,7},{7,8},{8,9},{9,10},{10,1... | collective-permute-start | bytes 24584 | tf_op jit(solution)/shard_map/ppermute | solution.py:17
  45.7 31.0 %collective-permute-start.1 = (bf16[2,4,1,512]{3,1,0,2:T(4,128)(2,1)S(1)}, bf16[2,4,1,512]{3,1,0,2:T(4,128)(2,1)S(1)}, u32[]{:S(2)}, u32[]{:S(2)}) collective-permute-start(bf16[2,4,1,512]{3,1,0,2:T(4,128)(2,1)S(1)} %get-tuple-element.24), channel_id=1, source_target_pairs={{1,0},{2,1},{3,2},{4,3},{5,4},{6,5},{7,6},{8,7},{9,8},{10,9},{11,1... | collective-permute-start | bytes 24584 | tf_op jit(solution)/shard_map/ppermute | solution.py:19
  48.1 16.2 %collective-permute-start.2 = (f32[1,2,4,64]{3,2,1,0:T(4,128)S(1)}, f32[1,2,4,64]{3,2,1,0:T(4,128)S(1)}, u32[]{:S(2)}, u32[]{:S(2)}) collective-permute-start(f32[1,2,4,64]{3,2,1,0:T(4,128)S(1)} %fusion.165), channel_id=1, source_target_pairs={{0,15},{1,0},{2,1},{3,2},{4,3},{5,4},{6,5},{7,6},{8,7},{9,8},{10,9... | collective-permute-start | bytes 6152 | tf_op jit(solution)/shard_map/ppermute | solution.py:70
  63.2 77.8 %copy-start.2 = (bf16[1,2,64,512]{3,2,1,0:T(8,128)(2,1)S(1)}, bf16[1,2,64,512]{3,2,1,0:T(8,128)(2,1)}, u32[]{:S(2)}) copy-start(bf16[1,2,64,512]{3,2,1,0:T(8,128)(2,1)} %param.17) | copy-start | bytes 393220
  64.3 2.0 collective-permute-start.3
  65.2 156.0 %copy-start.1 = (bf16[1,2,64,512]{3,2,1,0:T(8,128)(2,1)S(1)}, bf16[1,2,64,512]{3,2,1,0:T(8,128)(2,1)}, u32[]{:S(2)}) copy-start(bf16[1,2,64,512]{3,2,1,0:T(8,128)(2,1)} %param.16) | copy-start | bytes 393220
  66.3 5.7 %collective-permute-start.4 = (f32[1,2,4,64]{3,2,1,0:T(4,128)S(1)}, f32[1,2,4,64]{3,2,1,0:T(4,128)S(1)}, u32[]{:S(2)}, u32[]{:S(2)}) collective-permute-start(f32[1,2,4,64]{3,2,1,0:T(4,128)S(1)} %collective-permute-done.3), channel_id=1, source_target_pairs={{0,15},{1,0},{2,1},{3,2},{4,3},{5,4},{6,5},{7,6},{8,7},{9,8},{10,9... | collective-permute-start | bytes 6152 | tf_op jit(solution)/shard_map/ppermute | solution.py:70
  72.0 6.1 %collective-permute-start.5 = (f32[1,2,4,64]{3,2,1,0:T(4,128)S(1)}, f32[1,2,4,64]{3,2,1,0:T(4,128)S(1)}, u32[]{:S(2)}, u32[]{:S(2)}) collective-permute-start(f32[1,2,4,64]{3,2,1,0:T(4,128)S(1)} %collective-permute-done.4), channel_id=1, source_target_pairs={{0,15},{1,0},{2,1},{3,2},{4,3},{5,4},{6,5},{7,6},{8,7},{9,8},{10,9... | collective-permute-start | bytes 6152 | tf_op jit(solution)/shard_map/ppermute | solution.py:70
  78.1 5.3 %collective-permute-start.6 = (f32[1,2,4,64]{3,2,1,0:T(4,128)S(1)}, f32[1,2,4,64]{3,2,1,0:T(4,128)S(1)}, u32[]{:S(2)}, u32[]{:S(2)}) collective-permute-start(f32[1,2,4,64]{3,2,1,0:T(4,128)S(1)} %collective-permute-done.5), channel_id=1, source_target_pairs={{0,15},{1,0},{2,1},{3,2},{4,3},{5,4},{6,5},{7,6},{8,7},{9,8},{10,9... | collective-permute-start | bytes 6152 | tf_op jit(solution)/shard_map/ppermute | solution.py:70
  83.5 5.7 %collective-permute-start.7 = (f32[1,2,4,64]{3,2,1,0:T(4,128)S(1)}, f32[1,2,4,64]{3,2,1,0:T(4,128)S(1)}, u32[]{:S(2)}, u32[]{:S(2)}) collective-permute-start(f32[1,2,4,64]{3,2,1,0:T(4,128)S(1)} %collective-permute-done.6), channel_id=1, source_target_pairs={{0,15},{1,0},{2,1},{3,2},{4,3},{5,4},{6,5},{7,6},{8,7},{9,8},{10,9... | collective-permute-start | bytes 6152 | tf_op jit(solution)/shard_map/ppermute | solution.py:70
  89.2 5.7 %collective-permute-start.8 = (f32[1,2,4,64]{3,2,1,0:T(4,128)S(1)}, f32[1,2,4,64]{3,2,1,0:T(4,128)S(1)}, u32[]{:S(2)}, u32[]{:S(2)}) collective-permute-start(f32[1,2,4,64]{3,2,1,0:T(4,128)S(1)} %collective-permute-done.7), channel_id=1, source_target_pairs={{0,15},{1,0},{2,1},{3,2},{4,3},{5,4},{6,5},{7,6},{8,7},{9,8},{10,9... | collective-permute-start | bytes 6152 | tf_op jit(solution)/shard_map/ppermute | solution.py:70
  95.0 5.7 %collective-permute-start.9 = (f32[1,2,4,64]{3,2,1,0:T(4,128)S(1)}, f32[1,2,4,64]{3,2,1,0:T(4,128)S(1)}, u32[]{:S(2)}, u32[]{:S(2)}) collective-permute-start(f32[1,2,4,64]{3,2,1,0:T(4,128)S(1)} %collective-permute-done.8), channel_id=1, source_target_pairs={{0,15},{1,0},{2,1},{3,2},{4,3},{5,4},{6,5},{7,6},{8,7},{9,8},{10,9... | collective-permute-start | bytes 6152 | tf_op jit(solution)/shard_map/ppermute | solution.py:70
  100.7 5.7 %collective-permute-start.10 = (f32[1,2,4,64]{3,2,1,0:T(4,128)S(1)}, f32[1,2,4,64]{3,2,1,0:T(4,128)S(1)}, u32[]{:S(2)}, u32[]{:S(2)}) collective-permute-start(f32[1,2,4,64]{3,2,1,0:T(4,128)S(1)} %collective-permute-done.9), channel_id=1, source_target_pairs={{0,15},{1,0},{2,1},{3,2},{4,3},{5,4},{6,5},{7,6},{8,7},{9,8},{10,9... | collective-permute-start | bytes 6152 | tf_op jit(solution)/shard_map/ppermute | solution.py:70
  106.4 5.7 %collective-permute-start.11 = (f32[1,2,4,64]{3,2,1,0:T(4,128)S(1)}, f32[1,2,4,64]{3,2,1,0:T(4,128)S(1)}, u32[]{:S(2)}, u32[]{:S(2)}) collective-permute-start(f32[1,2,4,64]{3,2,1,0:T(4,128)S(1)} %collective-permute-done.10), channel_id=1, source_target_pairs={{0,15},{1,0},{2,1},{3,2},{4,3},{5,4},{6,5},{7,6},{8,7},{9,8},{10,9... | collective-permute-start | bytes 6152 | tf_op jit(solution)/shard_map/ppermute | solution.py:70
  112.1 5.7 %collective-permute-start.12 = (f32[1,2,4,64]{3,2,1,0:T(4,128)S(1)}, f32[1,2,4,64]{3,2,1,0:T(4,128)S(1)}, u32[]{:S(2)}, u32[]{:S(2)}) collective-permute-start(f32[1,2,4,64]{3,2,1,0:T(4,128)S(1)} %collective-permute-done.11), channel_id=1, source_target_pairs={{0,15},{1,0},{2,1},{3,2},{4,3},{5,4},{6,5},{7,6},{8,7},{9,8},{10,9... | collective-permute-start | bytes 6152 | tf_op jit(solution)/shard_map/ppermute | solution.py:70
  117.9 5.7 %collective-permute-start.13 = (f32[1,2,4,64]{3,2,1,0:T(4,128)S(1)}, f32[1,2,4,64]{3,2,1,0:T(4,128)S(1)}, u32[]{:S(2)}, u32[]{:S(2)}) collective-permute-start(f32[1,2,4,64]{3,2,1,0:T(4,128)S(1)} %collective-permute-done.12), channel_id=1, source_target_pairs={{0,15},{1,0},{2,1},{3,2},{4,3},{5,4},{6,5},{7,6},{8,7},{9,8},{10,9... | collective-permute-start | bytes 6152 | tf_op jit(solution)/shard_map/ppermute | solution.py:70
  123.6 5.7 %collective-permute-start.14 = (f32[1,2,4,64]{3,2,1,0:T(4,128)S(1)}, f32[1,2,4,64]{3,2,1,0:T(4,128)S(1)}, u32[]{:S(2)}, u32[]{:S(2)}) collective-permute-start(f32[1,2,4,64]{3,2,1,0:T(4,128)S(1)} %collective-permute-done.13), channel_id=1, source_target_pairs={{0,15},{1,0},{2,1},{3,2},{4,3},{5,4},{6,5},{7,6},{8,7},{9,8},{10,9... | collective-permute-start | bytes 6152 | tf_op jit(solution)/shard_map/ppermute | solution.py:70
  129.3 5.7 %collective-permute-start.15 = (f32[1,2,4,64]{3,2,1,0:T(4,128)S(1)}, f32[1,2,4,64]{3,2,1,0:T(4,128)S(1)}, u32[]{:S(2)}, u32[]{:S(2)}) collective-permute-start(f32[1,2,4,64]{3,2,1,0:T(4,128)S(1)} %collective-permute-done.14), channel_id=1, source_target_pairs={{0,15},{1,0},{2,1},{3,2},{4,3},{5,4},{6,5},{7,6},{8,7},{9,8},{10,9... | collective-permute-start | bytes 6152 | tf_op jit(solution)/shard_map/ppermute | solution.py:70
  135.1 5.7 %collective-permute-start.16 = (f32[1,2,4,64]{3,2,1,0:T(4,128)S(1)}, f32[1,2,4,64]{3,2,1,0:T(4,128)S(1)}, u32[]{:S(2)}, u32[]{:S(2)}) collective-permute-start(f32[1,2,4,64]{3,2,1,0:T(4,128)S(1)} %collective-permute-done.15), channel_id=1, source_target_pairs={{0,15},{1,0},{2,1},{3,2},{4,3},{5,4},{6,5},{7,6},{8,7},{9,8},{10,9... | collective-permute-start | bytes 6152 | tf_op jit(solution)/shard_map/ppermute | solution.py:70
  221.4 25.3 %collective-permute-start.18 = (bf16[2,4,1,512]{3,1,0,2:T(4,128)(2,1)S(1)}, bf16[2,4,1,512]{3,1,0,2:T(4,128)(2,1)S(1)}, u32[]{:S(2)}, u32[]{:S(2)}) collective-permute-start(bf16[2,4,1,512]{3,1,0,2:T(4,128)(2,1)S(1)} %get-tuple-element.22), channel_id=1, source_target_pairs={{1,0},{2,1},{3,2},{4,3},{5,4},{6,5},{7,6},{8,7},{9,8},{10,9},{11,1... | collective-permute-start | bytes 24584 | tf_op jit(solution)/shard_map/ppermute | solution.py:19
  222.7 12.2 %collective-permute-start.19 = (f32[1,2,4,64]{3,2,1,0:T(4,128)S(1)}, f32[1,2,4,64]{3,2,1,0:T(4,128)S(1)}, u32[]{:S(2)}, u32[]{:S(2)}) collective-permute-start(f32[1,2,4,64]{3,2,1,0:T(4,128)S(1)} %fusion.164), channel_id=1, source_target_pairs={{0,15},{1,0},{2,1},{3,2},{4,3},{5,4},{6,5},{7,6},{8,7},{9,8},{10,9... | collective-permute-start | bytes 6152 | tf_op jit(solution)/shard_map/ppermute | solution.py:70
  232.8 13.8 %collective-permute-start.17 = (bf16[2,4,1,512]{3,1,0,2:T(4,128)(2,1)S(1)}, bf16[2,4,1,512]{3,1,0,2:T(4,128)(2,1)S(1)}, u32[]{:S(2)}, u32[]{:S(2)}) collective-permute-start(bf16[2,4,1,512]{3,1,0,2:T(4,128)(2,1)S(1)} %get-tuple-element.22), channel_id=1, source_target_pairs={{0,1},{1,2},{2,3},{3,4},{4,5},{5,6},{6,7},{7,8},{8,9},{9,10},{10,1... | collective-permute-start | bytes 24584 | tf_op jit(solution)/shard_map/ppermute | solution.py:17
  234.9 1.3 collective-permute-start.20
  236.2 5.7 %collective-permute-start.21 = (f32[1,2,4,64]{3,2,1,0:T(4,128)S(1)}, f32[1,2,4,64]{3,2,1,0:T(4,128)S(1)}, u32[]{:S(2)}, u32[]{:S(2)}) collective-permute-start(f32[1,2,4,64]{3,2,1,0:T(4,128)S(1)} %collective-permute-done.20), channel_id=1, source_target_pairs={{0,15},{1,0},{2,1},{3,2},{4,3},{5,4},{6,5},{7,6},{8,7},{9,8},{10,9... | collective-permute-start | bytes 6152 | tf_op jit(solution)/shard_map/ppermute | solution.py:70
  242.0 6.1 %collective-permute-start.22 = (f32[1,2,4,64]{3,2,1,0:T(4,128)S(1)}, f32[1,2,4,64]{3,2,1,0:T(4,128)S(1)}, u32[]{:S(2)}, u32[]{:S(2)}) collective-permute-start(f32[1,2,4,64]{3,2,1,0:T(4,128)S(1)} %collective-permute-done.21), channel_id=1, source_target_pairs={{0,15},{1,0},{2,1},{3,2},{4,3},{5,4},{6,5},{7,6},{8,7},{9,8},{10,9... | collective-permute-start | bytes 6152 | tf_op jit(solution)/shard_map/ppermute | solution.py:70
  248.1 5.4 %collective-permute-start.23 = (f32[1,2,4,64]{3,2,1,0:T(4,128)S(1)}, f32[1,2,4,64]{3,2,1,0:T(4,128)S(1)}, u32[]{:S(2)}, u32[]{:S(2)}) collective-permute-start(f32[1,2,4,64]{3,2,1,0:T(4,128)S(1)} %collective-permute-done.22), channel_id=1, source_target_pairs={{0,15},{1,0},{2,1},{3,2},{4,3},{5,4},{6,5},{7,6},{8,7},{9,8},{10,9... | collective-permute-start | bytes 6152 | tf_op jit(solution)/shard_map/ppermute | solution.py:70
  253.4 5.7 %collective-permute-start.24 = (f32[1,2,4,64]{3,2,1,0:T(4,128)S(1)}, f32[1,2,4,64]{3,2,1,0:T(4,128)S(1)}, u32[]{:S(2)}, u32[]{:S(2)}) collective-permute-start(f32[1,2,4,64]{3,2,1,0:T(4,128)S(1)} %collective-permute-done.23), channel_id=1, source_target_pairs={{0,15},{1,0},{2,1},{3,2},{4,3},{5,4},{6,5},{7,6},{8,7},{9,8},{10,9... | collective-permute-start | bytes 6152 | tf_op jit(solution)/shard_map/ppermute | solution.py:70
  259.2 5.7 %collective-permute-start.25 = (f32[1,2,4,64]{3,2,1,0:T(4,128)S(1)}, f32[1,2,4,64]{3,2,1,0:T(4,128)S(1)}, u32[]{:S(2)}, u32[]{:S(2)}) collective-permute-start(f32[1,2,4,64]{3,2,1,0:T(4,128)S(1)} %collective-permute-done.24), channel_id=1, source_target_pairs={{0,15},{1,0},{2,1},{3,2},{4,3},{5,4},{6,5},{7,6},{8,7},{9,8},{10,9... | collective-permute-start | bytes 6152 | tf_op jit(solution)/shard_map/ppermute | solution.py:70
  264.9 5.7 %collective-permute-start.26 = (f32[1,2,4,64]{3,2,1,0:T(4,128)S(1)}, f32[1,2,4,64]{3,2,1,0:T(4,128)S(1)}, u32[]{:S(2)}, u32[]{:S(2)}) collective-permute-start(f32[1,2,4,64]{3,2,1,0:T(4,128)S(1)} %collective-permute-done.25), channel_id=1, source_target_pairs={{0,15},{1,0},{2,1},{3,2},{4,3},{5,4},{6,5},{7,6},{8,7},{9,8},{10,9... | collective-permute-start | bytes 6152 | tf_op jit(solution)/shard_map/ppermute | solution.py:70
  270.6 5.7 %collective-permute-start.27 = (f32[1,2,4,64]{3,2,1,0:T(4,128)S(1)}, f32[1,2,4,64]{3,2,1,0:T(4,128)S(1)}, u32[]{:S(2)}, u32[]{:S(2)}) collective-permute-start(f32[1,2,4,64]{3,2,1,0:T(4,128)S(1)} %collective-permute-done.26), channel_id=1, source_target_pairs={{0,15},{1,0},{2,1},{3,2},{4,3},{5,4},{6,5},{7,6},{8,7},{9,8},{10,9... | collective-permute-start | bytes 6152 | tf_op jit(solution)/shard_map/ppermute | solution.py:70
  276.4 5.7 %collective-permute-start.28 = (f32[1,2,4,64]{3,2,1,0:T(4,128)S(1)}, f32[1,2,4,64]{3,2,1,0:T(4,128)S(1)}, u32[]{:S(2)}, u32[]{:S(2)}) collective-permute-start(f32[1,2,4,64]{3,2,1,0:T(4,128)S(1)} %collective-permute-done.27), channel_id=1, source_target_pairs={{0,15},{1,0},{2,1},{3,2},{4,3},{5,4},{6,5},{7,6},{8,7},{9,8},{10,9... | collective-permute-start | bytes 6152 | tf_op jit(solution)/shard_map/ppermute | solution.py:70
  282.1 5.7 %collective-permute-start.29 = (f32[1,2,4,64]{3,2,1,0:T(4,128)S(1)}, f32[1,2,4,64]{3,2,1,0:T(4,128)S(1)}, u32[]{:S(2)}, u32[]{:S(2)}) collective-permute-start(f32[1,2,4,64]{3,2,1,0:T(4,128)S(1)} %collective-permute-done.28), channel_id=1, source_target_pairs={{0,15},{1,0},{2,1},{3,2},{4,3},{5,4},{6,5},{7,6},{8,7},{9,8},{10,9... | collective-permute-start | bytes 6152 | tf_op jit(solution)/shard_map/ppermute | solution.py:70
  287.8 5.7 %collective-permute-start.30 = (f32[1,2,4,64]{3,2,1,0:T(4,128)S(1)}, f32[1,2,4,64]{3,2,1,0:T(4,128)S(1)}, u32[]{:S(2)}, u32[]{:S(2)}) collective-permute-start(f32[1,2,4,64]{3,2,1,0:T(4,128)S(1)} %collective-permute-done.29), channel_id=1, source_target_pairs={{0,15},{1,0},{2,1},{3,2},{4,3},{5,4},{6,5},{7,6},{8,7},{9,8},{10,9... | collective-permute-start | bytes 6152 | tf_op jit(solution)/shard_map/ppermute | solution.py:70
  293.5 5.7 %collective-permute-start.31 = (f32[1,2,4,64]{3,2,1,0:T(4,128)S(1)}, f32[1,2,4,64]{3,2,1,0:T(4,128)S(1)}, u32[]{:S(2)}, u32[]{:S(2)}) collective-permute-start(f32[1,2,4,64]{3,2,1,0:T(4,128)S(1)} %collective-permute-done.30), channel_id=1, source_target_pairs={{0,15},{1,0},{2,1},{3,2},{4,3},{5,4},{6,5},{7,6},{8,7},{9,8},{10,9... | collective-permute-start | bytes 6152 | tf_op jit(solution)/shard_map/ppermute | solution.py:70
  299.3 5.7 %collective-permute-start.32 = (f32[1,2,4,64]{3,2,1,0:T(4,128)S(1)}, f32[1,2,4,64]{3,2,1,0:T(4,128)S(1)}, u32[]{:S(2)}, u32[]{:S(2)}) collective-permute-start(f32[1,2,4,64]{3,2,1,0:T(4,128)S(1)} %collective-permute-done.31), channel_id=1, source_target_pairs={{0,15},{1,0},{2,1},{3,2},{4,3},{5,4},{6,5},{7,6},{8,7},{9,8},{10,9... | collective-permute-start | bytes 6152 | tf_op jit(solution)/shard_map/ppermute | solution.py:70
  305.0 5.7 %collective-permute-start.33 = (f32[1,2,4,64]{3,2,1,0:T(4,128)S(1)}, f32[1,2,4,64]{3,2,1,0:T(4,128)S(1)}, u32[]{:S(2)}, u32[]{:S(2)}) collective-permute-start(f32[1,2,4,64]{3,2,1,0:T(4,128)S(1)} %collective-permute-done.32), channel_id=1, source_target_pairs={{0,15},{1,0},{2,1},{3,2},{4,3},{5,4},{6,5},{7,6},{8,7},{9,8},{10,9... | collective-permute-start | bytes 6152 | tf_op jit(solution)/shard_map/ppermute | solution.py:70
